TPU v7x, 128 devices: a whole 4x4x4 slice. The times are simulated.
128 devices in a mesh: dp: 32 (over z_hi, x, y), mp: 4 (over z_lo, core).
Axes of the slice: x: 4, y: 4, z: 4 (z_hi: 2, z_lo: 2; z = z_hi * 2 + z_lo), core: 2. Of those that a mesh axis runs over, the one named last changes fastest.
Arguments:
- sample_grad: bfloat16 [4608, 8192], P('dp', 'mp'), may hold values from -3 to 3
- advantage: int32 [4608], P('dp'), may hold values from 1024 to 8191
- route_rows: int32 [32, 144], P('dp'), may hold values from 0 to 143, each once within a row
- route_count: int32 [32, 32], P('dp'), may hold values from 1 to 4, 80 in all within a row
- gate_pre: bfloat16 [4096, 16384], P('mp', 'dp'), may hold values from -5 to 5
- up_pre: bfloat16 [4096, 16384], P('mp', 'dp'), may hold values from -5 to 5
- down_weight: bfloat16 [16384, 8192], P('dp', 'mp'), may hold values from -0.046875 to 0.046875
Outputs:
- grad_down: float32 [16384, 8192], P('dp', 'mp')
- grad_gate: bfloat16 [4096, 16384], P('mp', 'dp')
- grad_up: bfloat16 [4096, 16384], P('mp', 'dp')
Inputs may be any that keep to these rules, and one draw needn't show every extreme that they name: Each row of route_rows is a permutation of the sampler's 144 row numbers. `route_count`: each sampler sends every learner at least one row and 80 rows in all; in each sampler's row some learner receives exactly 4.
All inputs are finite; a program needn't handle non-finite values.
Results may differ from a plain program's by a relative error of at most 0.005.
Values may be sent and summed in bfloat16 or wider, within the bound.
No kernel may reach another device: no remote copies, remote signals or barrier semaphores. Data moves between devices by JAX's collectives and lax.ppermute only.
A program may use at most 128 MiB of HBM per device.

v0:
```python
import jax
import jax.numpy as jnp
from jax import lax
from jax.sharding import PartitionSpec as P

SLOTS = 128
LIVE = SLOTS * 5 // 8


def silu_parts(gate_in):
    sigmoid_val = jax.nn.sigmoid(gate_in)
    return (gate_in * sigmoid_val, sigmoid_val * (1.0 + gate_in * (1.0 - sigmoid_val)))


def mp_gather(hidden):
    n_mp = lax.axis_size("mp")
    half = n_mp // 2
    me = lax.axis_index("mp")
    far = lax.ppermute(hidden, "mp", [(i, (i + half) % n_mp) for i in range(n_mp)])
    pair = jnp.stack([hidden, far])
    near = lax.ppermute(pair, "mp", [(i, i ^ 1) for i in range(n_mp)])
    held = jnp.concatenate([pair, near])
    block = jnp.arange(n_mp, dtype=jnp.int32)
    where = jnp.where((block ^ me) % half == 0, 0, 1) * 2 + jnp.where(block ^ me >= half, 1, 0)
    return jnp.take(held, where, axis=0, mode="clip").reshape(
        n_mp * hidden.shape[0], hidden.shape[1]
    )


def dp_gather_small(block):
    n = lax.axis_size("dp")
    me = lax.axis_index("dp")
    held = block
    step = 1
    while step < n:
        theirs = lax.ppermute(held, "dp", [(i, i ^ step) for i in range(n)])
        low = me & step == 0
        held = jnp.where(low, jnp.concatenate([held, theirs]), jnp.concatenate([theirs, held]))
        step *= 2
    return held


def shards(sample_grad, advantage, route_rows, route_count, gate_pre, up_pre, down_weight):
    learners = lax.axis_size("dp")
    capacity = SLOTS // learners
    own = route_count[0]
    own_end = jnp.cumsum(own)
    pos = jnp.arange(LIVE, dtype=jnp.int32)
    before = own_end[None, :] <= pos[:, None]
    own_m = jnp.sum(before.astype(jnp.int32), axis=1)
    own_c = pos - jnp.sum(jnp.where(before, own[None, :], 0), axis=1)
    picked = route_rows[0][own_m * capacity + own_c]
    weights = advantage.astype(jnp.float32) * (1.0 / 4096.0)
    scaled = (sample_grad[picked].astype(jnp.float32) * weights[picked][:, None]).astype(
        jnp.bfloat16
    )
    sent, gate_late, up_late, own_late = lax.optimization_barrier(
        (scaled, gate_pre, up_pre, route_count)
    )
    gate_in = gate_late.astype(jnp.float32)
    up_in = up_late.astype(jnp.float32)
    activated, slopes = silu_parts(gate_in)
    hidden = (activated * up_in).astype(jnp.bfloat16)
    gathered = lax.all_gather(sent, "dp", axis=0, tiled=True)
    hidden_all = mp_gather(hidden)
    counts = dp_gather_small(own_late)
    everything = gathered
    ends = jnp.cumsum(counts, axis=1)
    starts = ends - counts
    done = ends[:, None, :] <= pos[None, :, None]
    m_of = jnp.sum(done.astype(jnp.int32), axis=2)
    c_of = pos[None, :] - jnp.sum(jnp.where(done, counts[:, None, :], 0), axis=2)
    sender = jnp.arange(learners, dtype=jnp.int32)[:, None]
    slot_of = (m_of * SLOTS + sender * capacity + c_of).reshape(-1)
    hidden_live = hidden_all[slot_of]
    everything, hidden_live = lax.optimization_barrier((everything, hidden_live))
    partial_live = lax.dot_general(
        everything, down_weight, (((1,), (1,)), ((), ())), preferred_element_type=jnp.float32
    )
    lane = jnp.arange(capacity, dtype=jnp.int32)
    live = (lane[None, None, :] < counts.T[:, :, None]).reshape(-1)
    first = jnp.arange(learners, dtype=jnp.int32)[None, :] * LIVE + starts.T
    source = jnp.where(live, (first[:, :, None] + lane[None, None, :]).reshape(-1), 0)
    me = lax.axis_index("mp")
    n_mp = lax.axis_size("mp")
    rows_per = hidden.shape[0]

    def partial_block(partial, b):
        return partial[lax.dynamic_slice_in_dim(source, b * rows_per, rows_per)]

    pairs_core = [(i, i ^ 1) for i in range(n_mp)]
    from_core = lax.ppermute(partial_block(partial_live, me ^ 3), "mp", pairs_core)
    to_chip = (partial_block(partial_live, me ^ 2) + from_core).astype(jnp.bfloat16)
    to_chip, partial_late = lax.optimization_barrier((to_chip, partial_live))
    from_chip = lax.ppermute(to_chip, "mp", [(i, i ^ 2) for i in range(n_mp)])
    from_core_own = lax.ppermute(partial_block(partial_late, me ^ 1), "mp", pairs_core)
    own_part = partial_block(partial_late, me)
    grad_down = lax.dot_general(
        hidden_live, everything, (((0,), (0,)), ((), ())), preferred_element_type=jnp.float32
    )
    hidden_grad = own_part + from_core_own + from_chip.astype(jnp.float32)
    hidden_grad = jnp.where(
        lax.dynamic_slice_in_dim(live, me * rows_per, rows_per)[:, None], hidden_grad, 0.0
    )
    grad_gate = (hidden_grad * up_in * slopes).astype(jnp.bfloat16)
    grad_up = (hidden_grad * activated).astype(jnp.bfloat16)
    return (grad_down, grad_gate, grad_up)


def solution(mesh):
    placed = (
        P("dp", "mp"),
        P("dp"),
        P("dp", None),
        P("dp", None),
        P("mp", "dp"),
        P("mp", "dp"),
        P("dp", "mp"),
    )
    return jax.shard_map(
        shards,
        mesh=mesh,
        in_specs=placed,
        out_specs=(P("dp", "mp"), P("mp", "dp"), P("mp", "dp")),
        check_vma=False,
    )
```

profile of v0, /device:TPU:1, one launch (start us, length us, event | category | flops | bytes accessed | tf_op | source)
XLA Modules:
  0.0 209.8 jit_solution(445629079293870821)
XLA Ops:
  7.2 0.0 copy-start
  7.2 0.0 copy-start.1
  7.2 0.0 all-gather.2.cloned.1.call-start
  7.2 0.9 convert_multiply_fusion.4
  8.1 0.7 copy.16
  8.8 0.1 reduce-window.8
  8.9 0.1 reduce
  9.0 0.7 convert_reduce_fusion.1
  9.8 1.6 gather_fusion
  11.4 1.3 gather_fusion.2
  12.7 0.0 copy-done.1
  12.7 0.8 gather_fusion.1
  13.5 0.0 copy-start.4
  13.5 0.8 multiply_convert_fusion.1
  14.4 0.0 all-gather.2.cloned.1.call-update
  14.4 2.2 %fusion = bf16[1024,512]{1,0:T(8,128)(2,1)S(1)} fusion(bf16[1024,512]{1,0:T(8,128)(2,1)} %param.12, bf16[1024,512]{1,0:T(8,128)(2,1)} %param.11), kind=kLoop, calls=%fused_computation.15 | loop fusion | flops 4194304 | bytes 3145728 | tf_op jit(solution)/shard_map/convert_element_type | solution.py:63
  16.6 2.5 %collective-permute-start = (bf16[1024,512]{1,0:T(8,128)(2,1)S(1)}, bf16[1024,512]{1,0:T(8,128)(2,1)}, u32[]{:S(2)}, u32[]{:S(2)}) collective-permute-start(bf16[1024,512]{1,0:T(8,128)(2,1)S(1)} %fusion), channel_id=1, source_target_pairs={{0,2},{1,3},{2,0},{3,1},{4,6},{5,7},{6,4},{7,5},{8,10},{9,11},{10,... | collective-permute-start | bytes 3145736 | tf_op jit(solution)/shard_map/ppermute | solution.py:19
  19.1 0.0 copy-done.4
  19.1 1.3 collective-permute-start.2
  20.5 1.5 collective-permute-done.2
  22.0 3.0 %collective-permute-start.3 = (s32[2,32]{1,0:T(2,128)S(1)}, s32[2,32]{1,0:T(2,128)S(1)}, u32[]{:S(2)}, u32[]{:S(2)}) collective-permute-start(s32[2,32]{1,0:T(2,128)S(1)} %add_select_fusion.5), channel_id=1, source_target_pairs={{0,8},{4,12},{8,0},{12,4},{16,24},{20,28},{24,16},{28,20},{32,40},... | collective-permute-start | bytes 776 | tf_op jit(solution)/shard_map/ppermute | solution.py:36
  25.0 1.0 collective-permute-done.3
  26.0 1.3 collective-permute-start.4
  27.3 17.2 %collective-permute-done = bf16[1024,512]{1,0:T(8,128)(2,1)} collective-permute-done((bf16[1024,512]{1,0:T(8,128)(2,1)S(1)}, bf16[1024,512]{1,0:T(8,128)(2,1)}, u32[]{:S(2)}, u32[]{:S(2)}) %collective-permute-start) | collective-permute-done | bytes 1048608 | tf_op jit(solution)/shard_map/ppermute | solution.py:19
  44.4 2.7 %pad_maximum_fusion.1 = bf16[2,1024,512]{2,1,0:T(8,128)(2,1)} fusion(bf16[1,1024,512]{2,1,0:T(8,128)(2,1)} %bitcast.9, bf16[1,1024,512]{2,1,0:T(8,128)(2,1)S(1)} %bitcast.31), kind=kLoop, calls=%fused_computation.23 | loop fusion | flops 1048576 | bytes 4194304 | tf_op jit(solution)/shard_map/stack | solution.py:20
  47.2 1.3 collective-permute-start.1
  48.4 0.0 collective-permute-done.4
  48.4 2.8 %collective-permute-start.5 = (s32[8,32]{1,0:T(8,128)S(1)}, s32[8,32]{1,0:T(8,128)S(1)}, u32[]{:S(2)}, u32[]{:S(2)}) collective-permute-start(s32[8,32]{1,0:T(8,128)S(1)} %add_select_fusion.3), channel_id=1, source_target_pairs={{0,32},{4,36},{8,40},{12,44},{16,48},{20,52},{24,56},{28,60},{32,0... | collective-permute-start | bytes 3080 | tf_op jit(solution)/shard_map/ppermute | solution.py:36
  51.3 1.2 collective-permute-done.5
  52.5 3.4 %collective-permute-start.6 = (s32[16,32]{1,0:T(8,128)S(1)}, s32[16,32]{1,0:T(8,128)S(1)}, u32[]{:S(2)}, u32[]{:S(2)}) collective-permute-start(s32[16,32]{1,0:T(8,128)S(1)} %add_select_fusion.2), channel_id=1, source_target_pairs={{0,64},{4,68},{8,72},{12,76},{16,80},{20,84},{24,88},{28,92},{32,9... | collective-permute-start | bytes 6152 | tf_op jit(solution)/shard_map/ppermute | solution.py:36
  55.9 1.7 collective-permute-done.6
  57.6 0.2 reduce_window_sum.18
  57.8 0.1 add_bitcast_fusion
  57.9 0.1 copy.18
  58.0 0.1 copy.17
  58.0 0.4 convert_reduce_fusion
  58.4 0.1 subtract_add_fusion
  58.5 0.1 add.173
  58.6 0.2 iota_compare_fusion
  58.8 0.3 lt.92
  59.2 1.0 iota_add_fusion
  60.1 1.3 add.182
  61.6 0.0 collective-permute-done.1
  61.6 3.6 %pad_maximum_fusion = bf16[4,1024,512]{2,1,0:T(8,128)(2,1)} fusion(bf16[2,1024,512]{2,1,0:T(8,128)(2,1)} %collective-permute-done.1, bf16[1,1024,512]{2,1,0:T(8,128)(2,1)} %bitcast.9, bf16[1,1024,512]{2,1,0:T(8,128)(2,1)S(1)} %bitcast.32), kind=kLoop, calls=%fused_computation.9 | loop fusion | flops 4194304 | bytes 8388608 | tf_op jit(solution)/shard_map/concatenate | solution.py:22
  65.2 5.1 %gather_fusion.3 = bf16[4,1024,512]{2,1,0:T(8,128)(2,1)} fusion(bf16[4,1024,512]{2,1,0:T(8,128)(2,1)} %pad_maximum_fusion, s32[1024]{0:T(1024)S(1)} %pad_clamp_fusion.1), kind=kCustom, calls=%fused_computation.3 | custom fusion | bytes 8388624 | tf_op jit(solution)/shard_map/jit(_take)/gather | solution.py:25
  70.3 11.1 %gather_fusion.4 = bf16[2560,512]{1,0:T(8,128)(2,1)} fusion(bf16[4096,512]{1,0:T(8,128)(2,1)} %bitcast.30, s32[3072]{0:T(1024)S(1)} %pad_clamp_fusion), kind=kCustom, calls=%fused_computation.4 | custom fusion | bytes 5253120 | tf_op jit(solution)/shard_map/gather | solution.py:75
  81.4 54.4 %all-gather.2.cloned.1.call-done = bf16[2560,2048]{1,0:T(8,128)(2,1)} async-done(((bf16[80,2048]{1,0:T(8,128)(2,1)}), bf16[2560,2048]{1,0:T(8,128)(2,1)}) %all-gather.2.cloned.1.call-update) | async-done | bytes 10485776 | tf_op jit(solution)/shard_map/all_gather | solution.py:64
  135.7 0.0 copy-done
  135.7 9.8 %fusion.21 = f32[2560,512]{1,0:T(8,128)} fusion(bf16[2560,2048]{1,0:T(8,128)(2,1)} %all-gather.2.cloned.1.call-done, bf16[512,2048]{1,0:T(8,128)(2,1)S(1)} %copy-done), kind=kOutput, calls=%fused_computation.77 | convolution fusion | flops 5368709120 | bytes 17825792 | tf_op jit(solution)/shard_map/dot_general | solution.py:77
  145.6 7.8 %gather_fusion.6 = f32[1024,512]{1,0:T(8,128)} fusion(f32[2560,512]{1,0:T(8,128)} %fusion.21, s32[1024]{0:T(1024)S(1)} %get-tuple-element.27), kind=kCustom, calls=%fused_computation.6 | custom fusion | bytes 4198400 | tf_op jit(solution)/shard_map/gather | solution.py:89
  153.4 1.4 collective-permute-start.7
  154.8 7.8 %gather_fusion.5 = f32[1024,512]{1,0:T(8,128)} fusion(f32[2560,512]{1,0:T(8,128)} %fusion.21, s32[1024]{0:T(1024)S(1)} %get-tuple-element.28), kind=kCustom, calls=%fused_computation.5 | custom fusion | bytes 4198400 | tf_op jit(solution)/shard_map/gather | solution.py:89
  162.5 0.0 collective-permute-done.7
  162.5 3.5 %add_convert_fusion = bf16[1024,512]{1,0:T(8,128)(2,1)} fusion(f32[1024,512]{1,0:T(8,128)} %gather_fusion.5, f32[1024,512]{1,0:T(8,128)} %collective-permute-done.7), kind=kLoop, calls=%fused_computation.26 | loop fusion | flops 1048576 | bytes 5242880 | tf_op jit(solution)/shard_map/convert_element_type | solution.py:93
  166.1 7.8 %gather_fusion.8 = f32[1024,512]{1,0:T(8,128)} fusion(f32[2560,512]{1,0:T(8,128)} %fusion.21, s32[1024]{0:T(1024)S(1)} %get-tuple-element.25), kind=kCustom, calls=%fused_computation.8 | custom fusion | bytes 4198400 | tf_op jit(solution)/shard_map/gather | solution.py:89
  173.8 0.0 collective-permute-start.8
  173.8 0.0 copy-done.3
  173.8 0.4 collective-permute-start.9
  174.2 10.4 %fusion.20 = f32[512,2048]{1,0:T(8,128)} fusion(bf16[2560,512]{1,0:T(8,128)(2,1)} %gather_fusion.4, bf16[2560,2048]{1,0:T(8,128)(2,1)} %all-gather.2.cloned.1.call-done), kind=kOutput, calls=%fused_computation.76 | convolution fusion | flops 5368709120 | bytes 17301504 | tf_op jit(solution)/shard_map/dot_general | solution.py:98
  184.6 7.9 %gather_fusion.7 = f32[1024,512]{1,0:T(8,128)} fusion(f32[2560,512]{1,0:T(8,128)} %fusion.21, s32[1024]{0:T(1024)S(1)} %get-tuple-element.26), kind=kCustom, calls=%fused_computation.7 | custom fusion | bytes 4198400 | tf_op jit(solution)/shard_map/gather | solution.py:89
  192.5 5.9 %collective-permute-done.9 = bf16[1024,512]{1,0:T(8,128)(2,1)} collective-permute-done((bf16[1024,512]{1,0:T(8,128)(2,1)}, bf16[1024,512]{1,0:T(8,128)(2,1)}, u32[]{:S(2)}, u32[]{:S(2)}) %collective-permute-start.9) | collective-permute-done | bytes 1048608 | tf_op jit(solution)/shard_map/ppermute | solution.py:95
  198.4 0.0 collective-permute-done.8
  198.4 0.0 copy-done.2
  198.4 4.6 %multiply_convert_fusion = (bf16[1024,512]{1,0:T(8,128)(2,1)}, bf16[1024,512]{1,0:T(8,128)(2,1)}) fusion(bf16[1024,512]{1,0:T(8,128)(2,1)} %param.11, bf16[1024,512]{1,0:T(8,128)(2,1)} %collective-permute-done.9, f32[1024,512]{1,0:T(8,128)} %gather_fusion.7, f32[1024,512]{1,0:T(8,128)} %collective-permute-done.8, pred[1024]{0:T(1024)(128)(4,1)S(1)} %dynamic-slice-done, ...), kind=kLoop, calls=%fused_computation.24 | loop fusion | flops 9961472 | bytes 9438208 | tf_op jit(solution)/shard_map/convert_element_type | solution.py:106
  (21 shorter events, 0.2 us)
Async XLA Ops:
  7.2 128.6 %copy-start = (bf16[512,2048]{1,0:T(8,128)(2,1)S(1)}, bf16[512,2048]{1,0:T(8,128)(2,1)}, u32[]{:S(2)}) copy-start(bf16[512,2048]{1,0:T(8,128)(2,1)} %param.13) | copy-start | bytes 6291460
  7.2 5.5 %copy-start.1 = (bf16[144,2048]{1,0:T(8,128)(2,1)S(1)}, bf16[144,2048]{1,0:T(8,128)(2,1)}, u32[]{:S(2)}) copy-start(bf16[144,2048]{1,0:T(8,128)(2,1)} %param.7) | copy-start | bytes 1769476
  7.2 128.5 %all-gather.2.cloned.1.call-start = ((), (), s32[]{:S(2)}) async-start(), calls=%async_computation | async-start | bytes 10813440 | tf_op jit(solution)/shard_map/all_gather | solution.py:64
  13.5 5.6 %copy-start.4 = (s32[1,32]{1,0:T(1,128)S(1)}, s32[1,32]{1,0:T(1,128)}, u32[]{:S(2)}) copy-start(s32[1,32]{1,0:T(1,128)} %param.10) | copy-start | bytes 388
  16.6 27.8 %collective-permute-start = (bf16[1024,512]{1,0:T(8,128)(2,1)S(1)}, bf16[1024,512]{1,0:T(8,128)(2,1)}, u32[]{:S(2)}, u32[]{:S(2)}) collective-permute-start(bf16[1024,512]{1,0:T(8,128)(2,1)S(1)} %fusion), channel_id=1, source_target_pairs={{0,2},{1,3},{2,0},{3,1},{4,6},{5,7},{6,4},{7,5},{8,10},{9,11},{10,... | collective-permute-start | bytes 3145736 | tf_op jit(solution)/shard_map/ppermute | solution.py:19
  19.1 2.8 %collective-permute-start.2 = (s32[1,32]{1,0:T(1,128)S(1)}, s32[1,32]{1,0:T(1,128)S(1)}, u32[]{:S(2)}, u32[]{:S(2)}) collective-permute-start(s32[1,32]{1,0:T(1,128)S(1)} %copy-done.4), channel_id=1, source_target_pairs={{0,4},{4,0},{8,12},{12,8},{16,20},{20,16},{24,28},{28,24},{32,36},... | collective-permute-start | bytes 392 | tf_op jit(solution)/shard_map/ppermute | solution.py:36
  22.0 4.0 %collective-permute-start.3 = (s32[2,32]{1,0:T(2,128)S(1)}, s32[2,32]{1,0:T(2,128)S(1)}, u32[]{:S(2)}, u32[]{:S(2)}) collective-permute-start(s32[2,32]{1,0:T(2,128)S(1)} %add_select_fusion.5), channel_id=1, source_target_pairs={{0,8},{4,12},{8,0},{12,4},{16,24},{20,28},{24,16},{28,20},{32,40},... | collective-permute-start | bytes 776 | tf_op jit(solution)/shard_map/ppermute | solution.py:36
  26.0 22.4 %collective-permute-start.4 = (s32[4,32]{1,0:T(4,128)S(1)}, s32[4,32]{1,0:T(4,128)S(1)}, u32[]{:S(2)}, u32[]{:S(2)}) collective-permute-start(s32[4,32]{1,0:T(4,128)S(1)} %add_select_fusion.4), channel_id=1, source_target_pairs={{0,16},{4,20},{8,24},{12,28},{16,0},{20,4},{24,8},{28,12},{32,48},... | collective-permute-start | bytes 1544 | tf_op jit(solution)/shard_map/ppermute | solution.py:36
  47.2 14.4 %collective-permute-start.1 = (bf16[2,1024,512]{2,1,0:T(8,128)(2,1)}, bf16[2,1024,512]{2,1,0:T(8,128)(2,1)}, u32[]{:S(2)}, u32[]{:S(2)}) collective-permute-start(bf16[2,1024,512]{2,1,0:T(8,128)(2,1)} %pad_maximum_fusion.1), channel_id=1, source_target_pairs={{0,1},{1,0},{2,3},{3,2},{4,5},{5,4},{6,7},{7,6},{8,9},{9,8},{10,11... | collective-permute-start | bytes 6291464 | tf_op jit(solution)/shard_map/ppermute | solution.py:21
  48.4 4.0 %collective-permute-start.5 = (s32[8,32]{1,0:T(8,128)S(1)}, s32[8,32]{1,0:T(8,128)S(1)}, u32[]{:S(2)}, u32[]{:S(2)}) collective-permute-start(s32[8,32]{1,0:T(8,128)S(1)} %add_select_fusion.3), channel_id=1, source_target_pairs={{0,32},{4,36},{8,40},{12,44},{16,48},{20,52},{24,56},{28,60},{32,0... | collective-permute-start | bytes 3080 | tf_op jit(solution)/shard_map/ppermute | solution.py:36
  52.5 5.2 %collective-permute-start.6 = (s32[16,32]{1,0:T(8,128)S(1)}, s32[16,32]{1,0:T(8,128)S(1)}, u32[]{:S(2)}, u32[]{:S(2)}) collective-permute-start(s32[16,32]{1,0:T(8,128)S(1)} %add_select_fusion.2), channel_id=1, source_target_pairs={{0,64},{4,68},{8,72},{12,76},{16,80},{20,84},{24,88},{28,92},{32,9... | collective-permute-start | bytes 6152 | tf_op jit(solution)/shard_map/ppermute | solution.py:36
  59.1 114.7 %copy-start.3 = (pred[4096]{0:T(1024)(128)(4,1)}, pred[4096]{0:T(1024)(128)(4,1)S(1)}, u32[]{:S(2)}) copy-start(pred[4096]{0:T(1024)(128)(4,1)S(1)} %lt.92) | copy-start | bytes 12292
  153.4 9.2 %collective-permute-start.7 = (f32[1024,512]{1,0:T(8,128)}, f32[1024,512]{1,0:T(8,128)}, u32[]{:S(2)}, u32[]{:S(2)}) collective-permute-start(f32[1024,512]{1,0:T(8,128)} %gather_fusion.6), channel_id=1, source_target_pairs={{0,1},{1,0},{2,3},{3,2},{4,5},{5,4},{6,7},{7,6},{8,9},{9,8},{10,11... | collective-permute-start | bytes 6291464 | tf_op jit(solution)/shard_map/ppermute | solution.py:92
  173.8 24.5 %collective-permute-start.8 = (f32[1024,512]{1,0:T(8,128)}, f32[1024,512]{1,0:T(8,128)}, u32[]{:S(2)}, u32[]{:S(2)}) collective-permute-start(f32[1024,512]{1,0:T(8,128)} %gather_fusion.8), channel_id=1, source_target_pairs={{0,1},{1,0},{2,3},{3,2},{4,5},{5,4},{6,7},{7,6},{8,9},{9,8},{10,11... | collective-permute-start | bytes 6291464 | tf_op jit(solution)/shard_map/ppermute | solution.py:96
  173.8 24.5 %collective-permute-start.9 = (bf16[1024,512]{1,0:T(8,128)(2,1)}, bf16[1024,512]{1,0:T(8,128)(2,1)}, u32[]{:S(2)}, u32[]{:S(2)}) collective-permute-start(bf16[1024,512]{1,0:T(8,128)(2,1)} %add_convert_fusion), channel_id=1, source_target_pairs={{0,2},{1,3},{2,0},{3,1},{4,6},{5,7},{6,4},{7,5},{8,10},{9,11},{10,... | collective-permute-start | bytes 3145736 | tf_op jit(solution)/shard_map/ppermute | solution.py:95
  184.6 13.7 %copy-start.2 = (bf16[1024,512]{1,0:T(8,128)(2,1)S(1)}, bf16[1024,512]{1,0:T(8,128)(2,1)}, u32[]{:S(2)}) copy-start(bf16[1024,512]{1,0:T(8,128)(2,1)} %param.12) | copy-start | bytes 3145732
  184.6 13.7 %dynamic-slice-start = ((pred[4096]{0:T(1024)(128)(4,1)}, s32[]{:T(128)}), pred[1024]{0:T(1024)(128)(4,1)S(1)}, s32[]{:S(2)}) async-start(pred[4096]{0:T(1024)(128)(4,1)} %copy-done.3, s32[]{:T(128)} %select_n.172), calls=%async_computation.1 | async-start | bytes 2560 | tf_op jit(solution)/shard_map/dynamic_slice | solution.py:103
Sparse Core Ops, SparseCore 0:
  14.5 121.1 all-gather.1
where the time goes:
time: 210 us
  waiting for transfers between devices  82.9 us (39%)
  local copies, waits for them, and re-layouts  53.7 us (26%)
  other arithmetic  21.4 us (10%)
  matrix products  20.2 us (10%)
  starting transfers between devices  17.4 us (8%)
  between operations  14.2 us (7%)
    all_gather x1, waiting for transfers between devices, shards(): gathered = lax.all_gather(sent, 'dp', axis=0, tiled=True)  54.4 us
    gather x4, local copies, waits for them, and re-layouts, partial_block(): return partial[lax.dynamic_slice_in_dim(source, b * rows_per, rows_per)]  31.2 us
    ppermute x1, waiting for transfers between devices, mp_gather(): lax.ppermute(hidden, 'mp', [(i, (i + half) % n_mp) for i in range(n_mp)])  17.2 us
    ppermute x5, starting transfers between devices, dp_gather_small(): theirs = lax.ppermute(held, 'dp', [(i, i ^ step) for i in range(n)])  11.8 us
    gather x1, local copies, waits for them, and re-layouts, shards(): hidden_live = hidden_all[slot_of]  11.1 us
    dot_general x1, matrix products, shards(): lax.dot_general(hidden_live, everything, (((0,), (0,)), ((), ())), prefer...  10.4 us
    dot_general x1, matrix products, shards(): lax.dot_general(everything, down_weight, (((1,), (1,)), ((), ())), prefer...  9.82 us
    ppermute x1, waiting for transfers between devices, shards(): from_chip = lax.ppermute(to_chip, 'mp', [(i, i ^ 2) for i in range(n_mp)])  5.87 us
  transfers between devices with their start and end apart: 11, of which 7 were waited for; matrix products, arithmetic and copies ran while one was open for 26% of the time, Pallas kernels for 0%

commit v1 on v0

--- a/solution.py
+++ b/solution.py
@@ -61,7 +61,9 @@
     up_in = up_late.astype(jnp.float32)
     activated, slopes = silu_parts(gate_in)
     hidden = (activated * up_in).astype(jnp.bfloat16)
-    gathered = lax.all_gather(sent, "dp", axis=0, tiled=True)
+    gathered = jnp.concatenate(
+        lax.all_to_all(jnp.stack([sent] * lax.axis_size("dp")), "dp", 0, 0), axis=0
+    )
     hidden_all = mp_gather(hidden)
     counts = dp_gather_small(own_late)
     everything = gathered

time: 210 us -> 286 us (1.36); the launches traced: 210 us -> 280 us
  waiting for transfers between devices: 82.9 us -> 136 us
  starting transfers between devices: 17.4 us -> 46.6 us
  between operations: 14.2 us -> 0.94 us
    ppermute x5, waiting for transfers between devices: 5.46 us -> 117 us  [dp_gather_small(): theirs = lax.ppermute(held, 'dp', [(i, i ^ step) for i in range(n)])]
    all_gather x1 -> x0, waiting for transfers between devices: 54.4 us -> none  [shards(): gathered = lax.all_gather(sent, 'dp', axis=0, tiled=True)]
    ppermute x5, starting transfers between devices: 11.8 us -> 28 us  [dp_gather_small(): theirs = lax.ppermute(held, 'dp', [(i, i ^ step) for i in range(n)])]
    all_to_all x0 -> x1, starting transfers between devices: none -> 11.3 us  [shards(): lax.all_to_all(jnp.stack([sent] * lax.axis_size('dp')), 'dp', 0, 0)]
    another operation x1 -> x2, local copies, waits for them, and re-layouts: 0.74 us -> 6.06 us  [the longest x1 5.16 us: shards(): jnp.stack([sent] * lax.axis_size('dp'))]
    ppermute x1, waiting for transfers between devices: 17.2 us -> 13.2 us  [mp_gather(): lax.ppermute(hidden, 'mp', [(i, (i + half) % n_mp) for i in range(n_mp)])]
  transfers between devices with their start and end apart: 11 -> 11, of which waited for: 7 -> 7; matrix products, arithmetic and copies ran while one was open for 26% -> 19% of each run, Pallas kernels for 0% -> 0%
where the time goes in v1:
time: 286 us; the launch traced here: 280 us
  waiting for transfers between devices  136 us (48%)
  local copies, waits for them, and re-layouts  56.3 us (20%)
  starting transfers between devices  46.6 us (16%)
  matrix products  20.2 us (7%)
  other arithmetic  20 us (7%)
    ppermute x5, waiting for transfers between devices, dp_gather_small(): theirs = lax.ppermute(held, 'dp', [(i, i ^ step) for i in range(n)])  117 us
    gather x4, local copies, waits for them, and re-layouts, partial_block(): return partial[lax.dynamic_slice_in_dim(source, b * rows_per, rows_per)]  28.6 us
    ppermute x5, starting transfers between devices, dp_gather_small(): theirs = lax.ppermute(held, 'dp', [(i, i ^ step) for i in range(n)])  28 us
    ppermute x1, waiting for transfers between devices, mp_gather(): lax.ppermute(hidden, 'mp', [(i, (i + half) % n_mp) for i in range(n_mp)])  13.2 us
    all_to_all x1, starting transfers between devices, shards(): lax.all_to_all(jnp.stack([sent] * lax.axis_size('dp')), 'dp', 0, 0)  11.3 us
    gather x1, local copies, waits for them, and re-layouts, shards(): hidden_live = hidden_all[slot_of]  11.1 us
    dot_general x1, matrix products, shards(): lax.dot_general(hidden_live, everything, (((0,), (0,)), ((), ())), prefer...  10.4 us
    dot_general x1, matrix products, shards(): lax.dot_general(everything, down_weight, (((1,), (1,)), ((), ())), prefer...  9.82 us
  transfers between devices with their start and end apart: 11, of which 7 were waited for; matrix products, arithmetic and copies ran while one was open for 19% of the time, Pallas kernels for 0%

profile of v1, /device:TPU:1, one launch (start us, length us, event | category | flops | bytes accessed | tf_op | source)
XLA Modules:
  0.0 280.4 jit_solution(11830865194639356219)
XLA Ops:
  0.6 0.0 copy-start
  0.6 0.0 copy-start.2
  0.7 0.9 copy.16
  1.6 0.1 reduce-window.8
  1.6 0.1 reduce
  1.7 0.7 convert_reduce_fusion.1
  2.5 1.6 gather_fusion
  4.2 0.7 convert_multiply_fusion.4
  4.8 0.0 copy-done.2
  4.8 0.8 gather_fusion.1
  5.6 1.3 gather_fusion.2
  6.9 0.1 multiply_convert_fusion.1
  7.0 5.2 %stack.8 = bf16[32,80,2048]{2,1,0:T(8,128)(2,1)} broadcast(bf16[80,2048]{1,0:T(8,128)(2,1)S(1)} %multiply_convert_fusion.1), dimensions={1,2} | broadcast | bytes 10813440 | tf_op jit(solution)/shard_map/stack | solution.py:65
  12.2 11.3 %all-to-all-start = ((bf16[32,80,2048]{2,1,0:T(8,128)(2,1)}), bf16[32,80,2048]{2,1,0:T(8,128)(2,1)}, u32[]{:S(2)}, u32[]{:S(2)}) async-start(bf16[32,80,2048]{2,1,0:T(8,128)(2,1)} %stack.8), calls=%async_computation | async-start | bytes 20971520 | tf_op jit(solution)/shard_map/all_to_all | solution.py:65
  23.5 0.0 copy-start.5
  23.5 2.2 fusion
  25.7 0.8 collective-permute-start
  26.5 0.0 copy-done.5
  26.5 1.2 collective-permute-start.2
  27.7 92.5 %collective-permute-done.2 = s32[1,32]{1,0:T(1,128)S(1)} collective-permute-done((s32[1,32]{1,0:T(1,128)S(1)}, s32[1,32]{1,0:T(1,128)S(1)}, u32[]{:S(2)}, u32[]{:S(2)}) %collective-permute-start.2) | collective-permute-done | bytes 160 | tf_op jit(solution)/shard_map/ppermute | solution.py:36
  120.3 16.9 %collective-permute-start.3 = (s32[2,32]{1,0:T(2,128)S(1)}, s32[2,32]{1,0:T(2,128)S(1)}, u32[]{:S(2)}, u32[]{:S(2)}) collective-permute-start(s32[2,32]{1,0:T(2,128)S(1)} %add_select_fusion.5), channel_id=1, source_target_pairs={{0,8},{4,12},{8,0},{12,4},{16,24},{20,28},{24,16},{28,20},{32,40},... | collective-permute-start | bytes 776 | tf_op jit(solution)/shard_map/ppermute | solution.py:36
  137.2 1.5 collective-permute-done.3
  138.7 0.1 collective-permute-start.4
  138.8 13.2 %collective-permute-done = bf16[1024,512]{1,0:T(8,128)(2,1)} collective-permute-done((bf16[1024,512]{1,0:T(8,128)(2,1)S(1)}, bf16[1024,512]{1,0:T(8,128)(2,1)}, u32[]{:S(2)}, u32[]{:S(2)}) %collective-permute-start) | collective-permute-done | bytes 1048608 | tf_op jit(solution)/shard_map/ppermute | solution.py:19
  152.0 2.7 pad_maximum_fusion.1
  154.7 1.5 collective-permute-start.1
  156.3 18.5 %collective-permute-done.4 = s32[4,32]{1,0:T(4,128)S(1)} collective-permute-done((s32[4,32]{1,0:T(4,128)S(1)}, s32[4,32]{1,0:T(4,128)S(1)}, u32[]{:S(2)}, u32[]{:S(2)}) %collective-permute-start.4) | collective-permute-done | bytes 544 | tf_op jit(solution)/shard_map/ppermute | solution.py:36
  174.8 9.8 %collective-permute-start.5 = (s32[8,32]{1,0:T(8,128)S(1)}, s32[8,32]{1,0:T(8,128)S(1)}, u32[]{:S(2)}, u32[]{:S(2)}) collective-permute-start(s32[8,32]{1,0:T(8,128)S(1)} %add_select_fusion.3), channel_id=1, source_target_pairs={{0,32},{4,36},{8,40},{12,44},{16,48},{20,52},{24,56},{28,60},{32,0... | collective-permute-start | bytes 3080 | tf_op jit(solution)/shard_map/ppermute | solution.py:36
  184.6 1.0 collective-permute-done.5
  185.6 0.0 collective-permute-start.6
  185.6 4.0 %collective-permute-done.6 = s32[16,32]{1,0:T(8,128)S(1)} collective-permute-done((s32[16,32]{1,0:T(8,128)S(1)}, s32[16,32]{1,0:T(8,128)S(1)}, u32[]{:S(2)}, u32[]{:S(2)}) %collective-permute-start.6) | collective-permute-done | bytes 2080 | tf_op jit(solution)/shard_map/ppermute | solution.py:36
  189.6 0.2 reduce_window_sum.18
  189.8 0.4 convert_reduce_fusion
  190.1 0.1 subtract_add_fusion
  190.2 0.1 add.173
  190.3 0.1 copy.17
  190.4 0.2 iota_compare_fusion
  190.6 0.3 lt.92
  190.9 0.0 copy-start.4
  190.9 0.1 add_bitcast_fusion
  191.0 0.1 copy.18
  191.1 1.0 iota_add_fusion
  192.1 1.3 add.182
  193.5 0.0 collective-permute-done.1
  193.5 3.6 %pad_maximum_fusion = bf16[4,1024,512]{2,1,0:T(8,128)(2,1)} fusion(bf16[2,1024,512]{2,1,0:T(8,128)(2,1)} %collective-permute-done.1, bf16[1,1024,512]{2,1,0:T(8,128)(2,1)} %bitcast.10, bf16[1,1024,512]{2,1,0:T(8,128)(2,1)S(1)} %bitcast.33), kind=kLoop, calls=%fused_computation.9 | loop fusion | flops 4194304 | bytes 8388608 | tf_op jit(solution)/shard_map/concatenate | solution.py:22
  197.1 5.0 %gather_fusion.3 = bf16[4,1024,512]{2,1,0:T(8,128)(2,1)} fusion(bf16[4,1024,512]{2,1,0:T(8,128)(2,1)} %pad_maximum_fusion, s32[1024]{0:T(1024)S(1)} %pad_clamp_fusion.1), kind=kCustom, calls=%fused_computation.3 | custom fusion | bytes 8388624 | tf_op jit(solution)/shard_map/jit(_take)/gather | solution.py:25
  202.0 11.1 %gather_fusion.4 = bf16[2560,512]{1,0:T(8,128)(2,1)} fusion(bf16[4096,512]{1,0:T(8,128)(2,1)} %bitcast.31, s32[3072]{0:T(1024)S(1)} %pad_clamp_fusion), kind=kCustom, calls=%fused_computation.4 | custom fusion | bytes 5253120 | tf_op jit(solution)/shard_map/gather | solution.py:77
  213.1 0.0 all-to-all-done
  213.1 9.8 %fusion.21 = f32[2560,512]{1,0:T(8,128)} fusion(bf16[2560,2048]{1,0:T(8,128)(2,1)} %bitcast.8, bf16[512,2048]{1,0:T(8,128)(2,1)S(1)} %copy-done), kind=kOutput, calls=%fused_computation.77 | convolution fusion | flops 5368709120 | bytes 17825792 | tf_op jit(solution)/shard_map/dot_general | solution.py:79
  223.0 7.8 %gather_fusion.6 = f32[1024,512]{1,0:T(8,128)} fusion(f32[2560,512]{1,0:T(8,128)} %fusion.21, s32[1024]{0:T(1024)S(1)} %get-tuple-element.27), kind=kCustom, calls=%fused_computation.6 | custom fusion | bytes 4198400 | tf_op jit(solution)/shard_map/gather | solution.py:91
  230.7 4.1 %collective-permute-start.7 = (f32[1024,512]{1,0:T(8,128)}, f32[1024,512]{1,0:T(8,128)}, u32[]{:S(2)}, u32[]{:S(2)}) collective-permute-start(f32[1024,512]{1,0:T(8,128)} %gather_fusion.6), channel_id=1, source_target_pairs={{0,1},{1,0},{2,3},{3,2},{4,5},{5,4},{6,7},{7,6},{8,9},{9,8},{10,11... | collective-permute-start | bytes 6291464 | tf_op jit(solution)/shard_map/ppermute | solution.py:94
  234.8 6.5 %gather_fusion.5 = f32[1024,512]{1,0:T(8,128)S(1)} fusion(f32[2560,512]{1,0:T(8,128)} %fusion.21, s32[1024]{0:T(1024)S(1)} %get-tuple-element.28), kind=kCustom, calls=%fused_computation.5 | custom fusion | bytes 4198400 | tf_op jit(solution)/shard_map/gather | solution.py:91
  241.3 0.0 collective-permute-done.7
  241.3 2.9 %add_convert_fusion = bf16[1024,512]{1,0:T(8,128)(2,1)} fusion(f32[1024,512]{1,0:T(8,128)S(1)} %gather_fusion.5, f32[1024,512]{1,0:T(8,128)} %collective-permute-done.7), kind=kLoop, calls=%fused_computation.26 | loop fusion | flops 1048576 | bytes 5242880 | tf_op jit(solution)/shard_map/convert_element_type | solution.py:95
  244.2 6.5 %gather_fusion.8 = f32[1024,512]{1,0:T(8,128)S(1)} fusion(f32[2560,512]{1,0:T(8,128)} %fusion.21, s32[1024]{0:T(1024)S(1)} %get-tuple-element.25), kind=kCustom, calls=%fused_computation.8 | custom fusion | bytes 4198400 | tf_op jit(solution)/shard_map/gather | solution.py:91
  250.7 0.1 collective-permute-start.8
  250.8 0.8 collective-permute-start.9
  251.7 10.4 %fusion.20 = f32[512,2048]{1,0:T(8,128)} fusion(bf16[2560,512]{1,0:T(8,128)(2,1)} %gather_fusion.4, bf16[2560,2048]{1,0:T(8,128)(2,1)} %bitcast.8), kind=kOutput, calls=%fused_computation.76 | convolution fusion | flops 5368709120 | bytes 17301504 | tf_op jit(solution)/shard_map/dot_general | solution.py:100
  262.1 7.9 %gather_fusion.7 = f32[1024,512]{1,0:T(8,128)} fusion(f32[2560,512]{1,0:T(8,128)} %fusion.21, s32[1024]{0:T(1024)S(1)} %get-tuple-element.26), kind=kCustom, calls=%fused_computation.7 | custom fusion | bytes 4198400 | tf_op jit(solution)/shard_map/gather | solution.py:91
  270.0 5.6 %collective-permute-done.9 = bf16[1024,512]{1,0:T(8,128)(2,1)} collective-permute-done((bf16[1024,512]{1,0:T(8,128)(2,1)}, bf16[1024,512]{1,0:T(8,128)(2,1)}, u32[]{:S(2)}, u32[]{:S(2)}) %collective-permute-start.9) | collective-permute-done | bytes 1048608 | tf_op jit(solution)/shard_map/ppermute | solution.py:97
  275.5 0.0 collective-permute-done.8
  275.6 0.0 copy-start.1
  275.6 4.7 %multiply_convert_fusion = (bf16[1024,512]{1,0:T(8,128)(2,1)}, bf16[1024,512]{1,0:T(8,128)(2,1)}) fusion(bf16[1024,512]{1,0:T(8,128)(2,1)} %param.11, bf16[1024,512]{1,0:T(8,128)(2,1)} %collective-permute-done.9, f32[1024,512]{1,0:T(8,128)} %gather_fusion.7, f32[1024,512]{1,0:T(8,128)} %collective-permute-done.8, pred[1024]{0:T(1024)(128)(4,1)S(1)} %dynamic-slice-done, ...), kind=kLoop, calls=%fused_computation.24 | loop fusion | flops 9961472 | bytes 9438208 | tf_op jit(solution)/shard_map/convert_element_type | solution.py:108
  280.3 0.0 copy-done.1
  (23 shorter events, 0.2 us)
Async XLA Ops:
  0.6 212.5 %copy-start = (bf16[512,2048]{1,0:T(8,128)(2,1)S(1)}, bf16[512,2048]{1,0:T(8,128)(2,1)}, u32[]{:S(2)}) copy-start(bf16[512,2048]{1,0:T(8,128)(2,1)} %param.13) | copy-start | bytes 6291460
  0.6 4.2 %copy-start.2 = (bf16[144,2048]{1,0:T(8,128)(2,1)S(1)}, bf16[144,2048]{1,0:T(8,128)(2,1)}, u32[]{:S(2)}) copy-start(bf16[144,2048]{1,0:T(8,128)(2,1)} %param.7) | copy-start | bytes 1769476
  12.2 200.9 %all-to-all-start = ((bf16[32,80,2048]{2,1,0:T(8,128)(2,1)}), bf16[32,80,2048]{2,1,0:T(8,128)(2,1)}, u32[]{:S(2)}, u32[]{:S(2)}) async-start(bf16[32,80,2048]{2,1,0:T(8,128)(2,1)} %stack.8), calls=%async_computation | async-start | bytes 20971520 | tf_op jit(solution)/shard_map/all_to_all | solution.py:65
  23.5 3.0 %copy-start.5 = (s32[1,32]{1,0:T(1,128)S(1)}, s32[1,32]{1,0:T(1,128)}, u32[]{:S(2)}) copy-start(s32[1,32]{1,0:T(1,128)} %param.10) | copy-start | bytes 388
  25.7 126.3 %collective-permute-start = (bf16[1024,512]{1,0:T(8,128)(2,1)S(1)}, bf16[1024,512]{1,0:T(8,128)(2,1)}, u32[]{:S(2)}, u32[]{:S(2)}) collective-permute-start(bf16[1024,512]{1,0:T(8,128)(2,1)S(1)} %fusion), channel_id=1, source_target_pairs={{0,2},{1,3},{2,0},{3,1},{4,6},{5,7},{6,4},{7,5},{8,10},{9,11},{10,... | collective-permute-start | bytes 3145736 | tf_op jit(solution)/shard_map/ppermute | solution.py:19
  26.5 93.7 %collective-permute-start.2 = (s32[1,32]{1,0:T(1,128)S(1)}, s32[1,32]{1,0:T(1,128)S(1)}, u32[]{:S(2)}, u32[]{:S(2)}) collective-permute-start(s32[1,32]{1,0:T(1,128)S(1)} %copy-done.5), channel_id=1, source_target_pairs={{0,4},{4,0},{8,12},{12,8},{16,20},{20,16},{24,28},{28,24},{32,36},... | collective-permute-start | bytes 392 | tf_op jit(solution)/shard_map/ppermute | solution.py:36
  120.3 18.4 %collective-permute-start.3 = (s32[2,32]{1,0:T(2,128)S(1)}, s32[2,32]{1,0:T(2,128)S(1)}, u32[]{:S(2)}, u32[]{:S(2)}) collective-permute-start(s32[2,32]{1,0:T(2,128)S(1)} %add_select_fusion.5), channel_id=1, source_target_pairs={{0,8},{4,12},{8,0},{12,4},{16,24},{20,28},{24,16},{28,20},{32,40},... | collective-permute-start | bytes 776 | tf_op jit(solution)/shard_map/ppermute | solution.py:36
  138.7 36.1 %collective-permute-start.4 = (s32[4,32]{1,0:T(4,128)S(1)}, s32[4,32]{1,0:T(4,128)S(1)}, u32[]{:S(2)}, u32[]{:S(2)}) collective-permute-start(s32[4,32]{1,0:T(4,128)S(1)} %add_select_fusion.4), channel_id=1, source_target_pairs={{0,16},{4,20},{8,24},{12,28},{16,0},{20,4},{24,8},{28,12},{32,48},... | collective-permute-start | bytes 1544 | tf_op jit(solution)/shard_map/ppermute | solution.py:36
  154.7 38.7 %collective-permute-start.1 = (bf16[2,1024,512]{2,1,0:T(8,128)(2,1)}, bf16[2,1024,512]{2,1,0:T(8,128)(2,1)}, u32[]{:S(2)}, u32[]{:S(2)}) collective-permute-start(bf16[2,1024,512]{2,1,0:T(8,128)(2,1)} %pad_maximum_fusion.1), channel_id=1, source_target_pairs={{0,1},{1,0},{2,3},{3,2},{4,5},{5,4},{6,7},{7,6},{8,9},{9,8},{10,11... | collective-permute-start | bytes 6291464 | tf_op jit(solution)/shard_map/ppermute | solution.py:21
  174.8 10.8 %collective-permute-start.5 = (s32[8,32]{1,0:T(8,128)S(1)}, s32[8,32]{1,0:T(8,128)S(1)}, u32[]{:S(2)}, u32[]{:S(2)}) collective-permute-start(s32[8,32]{1,0:T(8,128)S(1)} %add_select_fusion.3), channel_id=1, source_target_pairs={{0,32},{4,36},{8,40},{12,44},{16,48},{20,52},{24,56},{28,60},{32,0... | collective-permute-start | bytes 3080 | tf_op jit(solution)/shard_map/ppermute | solution.py:36
  185.6 4.0 %collective-permute-start.6 = (s32[16,32]{1,0:T(8,128)S(1)}, s32[16,32]{1,0:T(8,128)S(1)}, u32[]{:S(2)}, u32[]{:S(2)}) collective-permute-start(s32[16,32]{1,0:T(8,128)S(1)} %add_select_fusion.2), channel_id=1, source_target_pairs={{0,64},{4,68},{8,72},{12,76},{16,80},{20,84},{24,88},{28,92},{32,9... | collective-permute-start | bytes 6152 | tf_op jit(solution)/shard_map/ppermute | solution.py:36
  190.9 59.9 %copy-start.4 = (pred[4096]{0:T(1024)(128)(4,1)}, pred[4096]{0:T(1024)(128)(4,1)S(1)}, u32[]{:S(2)}) copy-start(pred[4096]{0:T(1024)(128)(4,1)S(1)} %lt.92) | copy-start | bytes 12292
  230.7 10.6 %collective-permute-start.7 = (f32[1024,512]{1,0:T(8,128)}, f32[1024,512]{1,0:T(8,128)}, u32[]{:S(2)}, u32[]{:S(2)}) collective-permute-start(f32[1024,512]{1,0:T(8,128)} %gather_fusion.6), channel_id=1, source_target_pairs={{0,1},{1,0},{2,3},{3,2},{4,5},{5,4},{6,7},{7,6},{8,9},{9,8},{10,11... | collective-permute-start | bytes 6291464 | tf_op jit(solution)/shard_map/ppermute | solution.py:94
  250.7 24.8 %collective-permute-start.8 = (f32[1024,512]{1,0:T(8,128)S(1)}, f32[1024,512]{1,0:T(8,128)}, u32[]{:S(2)}, u32[]{:S(2)}) collective-permute-start(f32[1024,512]{1,0:T(8,128)S(1)} %gather_fusion.8), channel_id=1, source_target_pairs={{0,1},{1,0},{2,3},{3,2},{4,5},{5,4},{6,7},{7,6},{8,9},{9,8},{10,11... | collective-permute-start | bytes 6291464 | tf_op jit(solution)/shard_map/ppermute | solution.py:98
  250.8 24.7 %collective-permute-start.9 = (bf16[1024,512]{1,0:T(8,128)(2,1)}, bf16[1024,512]{1,0:T(8,128)(2,1)}, u32[]{:S(2)}, u32[]{:S(2)}) collective-permute-start(bf16[1024,512]{1,0:T(8,128)(2,1)} %add_convert_fusion), channel_id=1, source_target_pairs={{0,2},{1,3},{2,0},{3,1},{4,6},{5,7},{6,4},{7,5},{8,10},{9,11},{10,... | collective-permute-start | bytes 3145736 | tf_op jit(solution)/shard_map/ppermute | solution.py:97
  262.1 13.5 %copy-start.3 = (bf16[1024,512]{1,0:T(8,128)(2,1)S(1)}, bf16[1024,512]{1,0:T(8,128)(2,1)}, u32[]{:S(2)}) copy-start(bf16[1024,512]{1,0:T(8,128)(2,1)} %param.12) | copy-start | bytes 3145732
  262.1 13.5 %dynamic-slice-start = ((pred[4096]{0:T(1024)(128)(4,1)}, s32[]{:T(128)}), pred[1024]{0:T(1024)(128)(4,1)S(1)}, s32[]{:S(2)}) async-start(pred[4096]{0:T(1024)(128)(4,1)} %copy-done.4, s32[]{:T(128)} %select_n.172), calls=%async_computation.1 | async-start | bytes 2560 | tf_op jit(solution)/shard_map/dynamic_slice | solution.py:105
  275.6 4.8 %copy-start.1 = (bf16[512,2048]{1,0:T(8,128)(2,1)S(1)}, bf16[512,2048]{1,0:T(8,128)(2,1)}, u32[]{:S(2)}) copy-start(bf16[512,2048]{1,0:T(8,128)(2,1)} %param.13) | copy-start | bytes 6291460
